TPU v7x, 32 devices: a whole 2x2x4 slice. The times are simulated.
32 devices in a mesh: section: 4 (over y, x), tp: 4 (over z), mirror: 2 (over core).
Axes of the slice: x: 2, y: 2, z: 4, core: 2. Of those that a mesh axis runs over, the one named last changes fastest.
Arguments:
- feats: bfloat16 [2, 2, 128, 5120], P('mirror', None, 'tp'), may hold values from -16 to 16
- types: int32 [2, 2, 128], P('mirror', None, 'tp'), may hold values from 0 to 63
- segs: int32 [2, 2, 5, 128], P('mirror'), may hold values from 0 to 3, never falling along the last dimension, each value on 1 to 64 neighbouring positions
- type_table: bfloat16 [64, 5120], replicated, may hold values from -3 to 3
- gains: float32 [2, 4, 5120], P('mirror', 'section'), may hold values from 0.25 to 1.75, as said below
- w_qkv: bfloat16 [2, 4, 3, 5120, 512], P('mirror', 'section', None, None, 'tp'), may hold values from -8 to 8, as said below
- w_out: bfloat16 [2, 4, 512, 5120], P('mirror', 'section', 'tp'), as said below
- carry_acts: bfloat16 [2, 4, 128, 5120], P('mirror', 'section', 'tp'), may hold values from -16 to 16
- grad_in: bfloat16 [2, 4, 128, 5120], P('mirror', 'section', 'tp'), may hold values from -6 to 6
- saved: bfloat16 [2, 4, 2, 128, 5120], P('mirror', 'section', None, 'tp'), may hold values from -16 to 16
- cotangent: bfloat16 [2, 2, 128, 5120], P('mirror', None, 'tp'), may hold values from -6 to 6
Outputs:
- acts: bfloat16 [2, 4, 2, 128, 5120], P('mirror', 'section', None, 'tp')
- grad_acts: bfloat16 [2, 4, 2, 128, 5120], P('mirror', 'section', None, 'tp')
- grad_qkv: bfloat16 [2, 4, 3, 5120, 512], P('mirror', 'section', None, None, 'tp')
- grad_out: bfloat16 [2, 4, 512, 5120], P('mirror', 'section', 'tp')
Inputs may be any that keep to these rules, and one draw needn't show every extreme that they name: w_qkv[1, k] equals w_qkv[0, 3 - k]. w_out[1, k] equals w_out[0, 3 - k]. gains[1, k] equals gains[0, 3 - k]. `segs`: segment numbers never fall along a micro-batch; each segment holds at most half of 128 tokens, and one holds exactly that many.
All inputs are finite; a program needn't handle non-finite values.
Results may differ from a plain program's by a relative error of at most 0.015.
Values may be sent and summed in bfloat16 or wider, within the bound.
No kernel may reach another device: no remote copies, remote signals or barrier semaphores. Data moves between devices by JAX's collectives and lax.ppermute only.
A program may use at most 128 MiB of HBM per device.

v0:
```python
import math
import numpy as np
import jax
import jax.numpy as jnp
from jax import lax
from jax.sharding import PartitionSpec as P

HD = 128


def passed_along(block, axis, distance):
    devices = range(lax.axis_size(axis))
    route = [(i - distance, i) for i in devices if i - distance in devices]
    return lax.ppermute(block, axis, route)


def flipped(value, axis, mask):
    return lax.ppermute(value, axis, [(i, i ^ mask) for i in range(lax.axis_size(axis))])


def normalize(values, gain_row):
    mean_square = jnp.mean(values * values, axis=-1, keepdims=True)
    return values * lax.rsqrt(mean_square + 1e-05) * gain_row


def segment_mask(segment_ids):
    position = jnp.arange(segment_ids.shape[0], dtype=jnp.int32)
    causal = position[None, :] <= position[:, None]
    return causal & (segment_ids[:, None] == segment_ids[None, :])


def attend(queries, keys_all, values_all, seg_mask):
    scores = jnp.einsum(
        "ihd,jhd->hij", queries, keys_all, preferred_element_type=jnp.float32
    ) / math.sqrt(queries.shape[-1])
    scores = jnp.where(seg_mask[None], scores, -1e30)
    highest = lax.stop_gradient(jnp.max(scores, axis=-1, keepdims=True))
    expo = jnp.exp(scores - highest)
    probs = (expo / jnp.sum(expo, axis=-1, keepdims=True)).astype(values_all.dtype)
    return jnp.einsum("hij,jhd->ihd", probs, values_all, preferred_element_type=jnp.float32)


def embedding(feat_rows, type_rows, type_table):
    onehot = (
        type_rows[:, None] == jnp.arange(type_table.shape[0], dtype=jnp.int32)[None, :]
    ).astype(jnp.bfloat16)
    looked = jnp.dot(onehot, type_table, preferred_element_type=jnp.float32)
    return (feat_rows.astype(jnp.float32) + looked).astype(jnp.bfloat16)


def gathered(blocks):
    full = lax.all_gather(jnp.stack(blocks), "tp", axis=1, tiled=True)
    return [full[i] for i in range(len(blocks))]


def scattered(blocks):
    part = lax.psum_scatter(jnp.stack(blocks), "tp", scatter_dimension=1, tiled=True)
    return [part[i] for i in range(len(blocks))]


def shards(
    feats, types, segs, type_table, gains, w_qkv, w_out, carry_acts, grad_in, saved, cotangent
):
    sections = lax.axis_size("section")
    section_index = lax.axis_index("section")
    on_first_pipe = lax.axis_index("mirror") == 0
    position = jnp.where(on_first_pipe, section_index, sections - 1 - section_index)
    gain_row = gains[0, 0]
    qkv_weight = w_qkv[0, 0]
    out_weight = w_out[0, 0]
    window_steps = feats.shape[1]
    seq_len = segs.shape[3]
    model_width = qkv_weight.shape[1]
    inner_here = qkv_weight.shape[-1]
    heads_here = inner_here // HD

    def mask_for(which, index):
        return segment_mask(lax.dynamic_index_in_dim(segs[0, which], index, 0, keepdims=False))

    def normed_rows(rows):
        return normalize(rows.astype(jnp.float32), gain_row).astype(jnp.bfloat16)

    def heads_of(normed_full):
        projected = jnp.einsum(
            "sd,cdn->csn", normed_full, qkv_weight, preferred_element_type=jnp.float32
        ).astype(jnp.bfloat16)
        return projected.reshape(3, seq_len, heads_here, HD)

    def forward_part(normed_full, seg_mask, heads_view=None):
        if heads_view is None:
            heads_view = heads_of(normed_full)
        mixed = (
            attend(heads_view[0], heads_view[1], heads_view[2], seg_mask)
            .reshape(seq_len, inner_here)
            .astype(jnp.bfloat16)
        )
        return mixed

    def backward_part(normed_full, upstream_full, seg_mask, heads_view=None):
        if heads_view is None:
            heads_view = heads_of(normed_full)
        primal, pull_attend = jax.vjp(
            lambda query_part, key_part, value_part: attend(
                query_part, key_part, value_part, seg_mask
            ),
            heads_view[0],
            heads_view[1],
            heads_view[2],
        )
        mixed = primal.reshape(seq_len, inner_here).astype(jnp.bfloat16)
        d_mixed = jnp.einsum(
            "sd,nd->sn", upstream_full, out_weight, preferred_element_type=jnp.float32
        ).astype(jnp.bfloat16)
        pulled = pull_attend(d_mixed.astype(jnp.float32).reshape(seq_len, heads_here, HD))
        d_projected = jnp.stack(pulled).reshape(3, seq_len, inner_here)
        return (d_projected, mixed)

    qkv_rows = jnp.transpose(qkv_weight, (0, 2, 1)).reshape(3 * inner_here, model_width)
    padded_out = jnp.concatenate(
        [out_weight, jnp.zeros((2 * inner_here, model_width), out_weight.dtype)], axis=0
    )
    block_weight = jnp.stack([qkv_rows, padded_out])

    def projected_back(d_projected, forward_mixed):
        lhs = jnp.stack(
            [
                jnp.transpose(d_projected, (1, 0, 2)).reshape(seq_len, 3 * inner_here),
                jnp.concatenate(
                    [forward_mixed, jnp.zeros((seq_len, 2 * inner_here), forward_mixed.dtype)],
                    axis=1,
                ),
            ]
        )
        return jnp.einsum(
            "tsk,tkd->tsd", lhs, block_weight, preferred_element_type=jnp.float32
        ).astype(jnp.bfloat16)

    def weight_terms(normed_fulls, d_projecteds, mixeds, upstream_fulls):
        qkv_sum = None
        out_sum = None
        for normed_full, d_projected, mixed, upstream_full in zip(
            normed_fulls, d_projecteds, mixeds, upstream_fulls
        ):
            qkv_term = jnp.einsum(
                "sd,csn->cdn", normed_full, d_projected, preferred_element_type=jnp.float32
            )
            out_term = jnp.einsum(
                "sn,sd->nd", mixed, upstream_full, preferred_element_type=jnp.float32
            )
            qkv_sum = qkv_term if qkv_sum is None else qkv_sum + qkv_term
            out_sum = out_term if out_sum is None else out_sum + out_term
        return (qkv_sum.astype(jnp.bfloat16), out_sum.astype(jnp.bfloat16))

    def input_grad(layer_in, upstream, d_normed):
        unused_norm, pull_norm = jax.vjp(
            lambda inputs: normalize(inputs, gain_row), layer_in.astype(jnp.float32)
        )
        d_input = pull_norm(d_normed.astype(jnp.float32))[0]
        return (upstream.astype(jnp.float32) + d_input).astype(jnp.bfloat16)

    pair_axes = ("section", "mirror")
    mirror_size = lax.axis_size("mirror")
    up_pairs = []
    down_pairs = []
    for section in range(sections):
        for mirror in range(mirror_size):
            ahead = 1 if mirror == 0 else -1
            if 0 <= section + ahead < sections:
                up_pairs.append(
                    (section * mirror_size + mirror, (section + ahead) * mirror_size + mirror)
                )
            if 0 <= section - ahead < sections:
                down_pairs.append(
                    (section * mirror_size + mirror, (section - ahead) * mirror_size + mirror)
                )
    bit_count = lax.axis_size(pair_axes).bit_length() - 1
    section_bits = list(range(1, bit_count))
    if section_bits:
        routes = []
        for start in range(len(section_bits)):
            order = section_bits[start:] + section_bits[:start]
            routes.append([1 | 1 << order[0]] + [1 << bit for bit in order[1:]])
    else:
        routes = [[1]]

    def to_partner(value):
        return flipped(value, pair_axes, (1 << bit_count) - 1)

    last_step = window_steps - 1
    saved_normed = [normed_rows(saved[0, 0, t]) for t in range(window_steps)]
    backward_normed_full = [None] * window_steps
    upstream_fulls = []
    d_projecteds = []
    mixeds = []
    partner_normed = [None] * window_steps
    partner_upstream = []
    partner_d_projected = []
    partner_mixed = []
    forward_outs = []
    backward_outs = []
    forward_in = carry_acts[0, 0]
    backward_in = grad_in[0, 0]
    inbox = {}
    deferred = {}
    tie_scatter = {}
    for step_index in range(window_steps):
        embedded = embedding(feats[0, step_index], types[0, step_index], type_table)
        current = jnp.where(position == 0, embedded, forward_in)
        upstream = jnp.where(position == sections - 1, cotangent[0, step_index], backward_in)
        if step_index == 0:
            upstream_full, backward_normed_full[0], forward_normed_full = gathered(
                [upstream, saved_normed[0], normed_rows(current)]
            )
            first_sent = to_partner(jnp.stack([upstream_full, backward_normed_full[0]]))
            paired = jnp.einsum(
                "tsd,cdn->tcsn",
                jnp.stack([backward_normed_full[0], forward_normed_full]),
                qkv_weight,
                preferred_element_type=jnp.float32,
            ).astype(jnp.bfloat16)
            step_heads = [paired[t].reshape(3, seq_len, heads_here, HD) for t in range(2)]
        else:
            step_heads = [None, None]
            upstream_full, forward_normed_full = gathered([upstream, normed_rows(current)])
            inbox[f"rows{step_index}"] = to_partner(upstream_full)
        d_projected, mixed = backward_part(
            backward_normed_full[step_index],
            upstream_full,
            mask_for(1, step_index + position),
            step_heads[0],
        )
        upstream_fulls.append(upstream_full)
        d_projecteds.append(d_projected)
        mixeds.append(mixed)
        small = jnp.concatenate([d_projected, mixed[None]])
        if step_index < last_step:
            deferred[f"small{step_index}"] = small
        else:
            inbox[f"small{step_index}"] = to_partner(small)
        forward_mixed = forward_part(
            forward_normed_full, mask_for(0, step_index - position + sections - 1), step_heads[1]
        )
        both_parts, tie_scatter = lax.optimization_barrier(
            (projected_back(d_projected, forward_mixed), tie_scatter)
        )
        inbox.update(tie_scatter)
        tie_scatter = {}
        both_rows = lax.psum_scatter(both_parts, "tp", scatter_dimension=1, tiled=True)
        d_normed, attn_rows = (both_rows[0], both_rows[1])
        if step_index == 0 and window_steps > 1:
            later_rows, d_normed = lax.optimization_barrier((saved_normed[1:], d_normed))
            later = gathered(later_rows)
            backward_normed_full[1:] = later
            deferred["later"] = jnp.stack(later)
        backward_out = input_grad(saved[0, 0, step_index], upstream, d_normed)
        forward_out = (current.astype(jnp.float32) + attn_rows.astype(jnp.float32)).astype(
            jnp.bfloat16
        )
        forward_outs.append(forward_out)
        backward_outs.append(backward_out)
        if step_index < last_step:
            backward_in = lax.ppermute(backward_out, pair_axes, down_pairs)
            forward_in = lax.ppermute(forward_out, pair_axes, up_pairs)
            if step_index == 0:
                deferred, first_sent, backward_in, forward_in = lax.optimization_barrier(
                    (deferred, first_sent, backward_in, forward_in)
                )
                inbox["first"] = first_sent
            else:
                deferred, backward_in, forward_in = lax.optimization_barrier(
                    (deferred, backward_in, forward_in)
                )
            tie_scatter = {key: to_partner(value) for key, value in deferred.items()}
            deferred = {}
    partner_upstream = [inbox["first"][0]] + [inbox[f"rows{t}"] for t in range(1, window_steps)]
    partner_normed = [inbox["first"][1]] + (
        [inbox["later"][t] for t in range(window_steps - 1)] if window_steps > 1 else []
    )
    partner_d_projected = [inbox[f"small{t}"][:3] for t in range(window_steps)]
    partner_mixed = [inbox[f"small{t}"][3] for t in range(window_steps)]
    own_qkv, own_out = weight_terms(backward_normed_full, d_projecteds, mixeds, upstream_fulls)
    other_qkv, other_out = weight_terms(
        partner_normed, partner_d_projected, partner_mixed, partner_upstream
    )
    grad_qkv = (own_qkv.astype(jnp.float32) + other_qkv.astype(jnp.float32)).astype(jnp.bfloat16)
    grad_out = (own_out.astype(jnp.float32) + other_out.astype(jnp.float32)).astype(jnp.bfloat16)
    acts_block = jnp.stack(forward_outs)[None, None]
    grads_block = jnp.stack(backward_outs)[None, None]
    return (acts_block, grads_block, grad_qkv[None, None], grad_out[None, None])


def solution(mesh):
    in_specs = (
        P("mirror", None, "tp", None),
        P("mirror", None, "tp"),
        P("mirror", None, None, None),
        P(),
        P("mirror", "section", None),
        P("mirror", "section", None, None, "tp"),
        P("mirror", "section", "tp", None),
        P("mirror", "section", "tp", None),
        P("mirror", "section", "tp", None),
        P("mirror", "section", None, "tp", None),
        P("mirror", None, "tp", None),
    )
    out_specs = (
        P("mirror", "section", None, "tp", None),
        P("mirror", "section", None, "tp", None),
        P("mirror", "section", None, None, "tp"),
        P("mirror", "section", "tp", None),
    )
    return jax.shard_map(shards, mesh=mesh, in_specs=in_specs, out_specs=out_specs, check_vma=False)
```

profile of v0, /device:TPU:0, one launch (start us, length us, event | category | flops | bytes accessed | tf_op | source)
XLA Modules:
  0.0 318.5 jit_solution(18364899609434030031)
XLA Ops:
  7.3 1.4 slice_bitcast_fusion.59
  8.7 1.5 multiply_reduce_fusion
  10.2 1.3 fusion.72
  11.7 0.9 fusion.91
  12.6 1.1 pad_maximum_fusion.3
  13.8 6.3 %copy.15 = bf16[3,128,5120]{2,1,0:T(8,128)(2,1)} copy(bf16[3,128,5120]{1,2,0:T(8,128)(2,1)} %bitcast.361) | data formatting | bytes 7864320 | tf_op jit(solution)/shard_map/transpose | solution.py:118
  20.1 0.5 fusion.123
  20.6 3.7 %pad_bitcast_fusion = bf16[1,384,5120]{2,1,0:T(8,128)(2,1)} fusion(bf16[128,5120]{1,0:T(8,128)(2,1)} %bitcast.363), kind=kLoop, calls=%fused_computation.28 | loop fusion | bytes 5242880 | tf_op jit(solution)/shard_map/stack | solution.py:122
  24.3 68.7 %all-gather.5.cloned.1.call-done = bf16[3,128,5120]{2,1,0:T(8,128)(2,1)} async-done(((bf16[3,32,5120]{2,1,0:T(8,128)(2,1)}), bf16[3,128,5120]{2,1,0:T(8,128)(2,1)}) %all-gather.5.cloned.1.call-update) | async-done | bytes 3932176 | tf_op jit(solution)/shard_map/all_gather | solution.py:52
  93.0 4.6 %fusion.33 = bf16[2,3,128,128]{3,2,1,0:T(8,128)(2,1)S(1)} fusion(bf16[1,1,3,5120,128]{4,3,2,1,0:T(8,128)(2,1)} %param.16, bf16[3,128,5120]{2,1,0:T(8,128)(2,1)} %all-gather.5.cloned.1.call-done), kind=kOutput, calls=%fused_computation.47 | convolution fusion | flops 1006731264 | bytes 6750208 | tf_op jit(solution)/shard_map/tsd,cdn->tcsn/dot_general | solution.py:215
  97.9 2.0 fusion.68
  100.2 0.2 fusion.59
  100.4 0.2 fusion.60
  100.6 0.2 fusion.61
  101.0 0.2 fusion.62
  101.3 3.0 convolution_convert_fusion.1
  104.3 1.3 fusion.9
  105.6 3.5 %stack.115 = bf16[2,128,5120]{2,1,0:T(8,128)(2,1)} slice(bf16[3,128,5120]{2,1,0:T(8,128)(2,1)} %all-gather.5.cloned.1.call-done), slice={[0:2], [0:128], [0:5120]} | slice | bytes 5242880 | tf_op jit(solution)/shard_map/stack | solution.py:214
  109.1 1.7 collective-permute-start
  110.8 44.5 %reduce-scatter.3.cloned.1.call-done = bf16[2,32,5120]{2,1,0:T(8,128)(2,1)} async-done(((bf16[2,128,5120]{2,1,0:T(8,128)(2,1)}), bf16[2,32,5120]{2,1,0:T(8,128)(2,1)}) %reduce-scatter.3.cloned.1.call-update) | async-done | bytes 655376 | tf_op jit(solution)/shard_map/reduce_scatter | solution.py:248
  155.2 1.0 slice_bitcast_fusion.24
  156.3 0.2 fusion.73
  156.6 0.3 fusion.78
  156.9 1.3 collective-permute-start.1
  158.2 1.0 fusion.90
  159.2 5.3 %collective-permute-start.2 = (bf16[32,5120]{1,0:T(8,128)(2,1)S(1)}, bf16[32,5120]{1,0:T(8,128)(2,1)}, u32[]{:S(2)}, u32[]{:S(2)}) collective-permute-start(bf16[32,5120]{1,0:T(8,128)(2,1)S(1)} %fusion.90), channel_id=1, source_target_pairs={{0,8},{8,16},{9,1},{16,24},{17,9},{25,17},{2,10},{10,18},{11,3},{1... | collective-permute-start | bytes 983048 | tf_op jit(solution)/shard_map/ppermute | solution.py:263
  164.5 0.9 convolution_convert_fusion.8
  165.5 0.7 pad_maximum_fusion.5
  166.1 3.3 %collective-permute-done = bf16[2,128,5120]{2,1,0:T(8,128)(2,1)} collective-permute-done((bf16[2,128,5120]{2,1,0:T(8,128)(2,1)}, bf16[2,128,5120]{2,1,0:T(8,128)(2,1)}, u32[]{:S(2)}, u32[]{:S(2)}) %collective-permute-start) | collective-permute-done | bytes 2621472 | tf_op jit(solution)/shard_map/ppermute | solution.py:18
  169.4 6.7 %collective-permute-done.1 = bf16[32,5120]{1,0:T(8,128)(2,1)S(1)} collective-permute-done((bf16[32,5120]{1,0:T(8,128)(2,1)S(1)}, bf16[32,5120]{1,0:T(8,128)(2,1)S(1)}, u32[]{:S(2)}, u32[]{:S(2)}) %collective-permute-start.1) | collective-permute-done | bytes 327712 | tf_op jit(solution)/shard_map/ppermute | solution.py:262
  176.1 13.3 %all-gather.9.cloned.1.call-done = bf16[128,5120]{1,0:T(8,128)(2,1)} async-done(((bf16[32,5120]{1,0:T(8,128)(2,1)}), bf16[128,5120]{1,0:T(8,128)(2,1)}) %all-gather.9.cloned.1.call-update) | async-done | bytes 1310736 | tf_op jit(solution)/shard_map/all_gather | solution.py:52
  189.5 0.2 fusion.79
  189.9 0.9 pad_maximum_fusion.4
  190.9 0.2 reduce-scatter.5.cloned.1.call-start
  191.1 1.2 collective-permute-start.3
  192.3 1.5 collective-permute-start.4
  193.8 3.0 fusion.44
  197.0 48.9 %all-gather.7.cloned.1.call-done = bf16[2,128,5120]{2,1,0:T(8,128)(2,1)} async-done(((bf16[2,32,5120]{2,1,0:T(8,128)(2,1)}), bf16[2,128,5120]{2,1,0:T(8,128)(2,1)}) %all-gather.7.cloned.1.call-update) | async-done | bytes 2621456 | tf_op jit(solution)/shard_map/all_gather | solution.py:52
  246.0 2.0 fusion.67
  248.1 3.5 %fusion.49 = bf16[3,128,128]{2,1,0:T(8,128)(2,1)S(1)} fusion(bf16[1,1,3,5120,128]{4,3,2,1,0:T(8,128)(2,1)} %param.16, bf16[2,128,5120]{2,1,0:T(8,128)(2,1)} %all-gather.7.cloned.1.call-done), kind=kOutput, calls=%fused_computation.55 | convolution fusion | flops 503365632 | bytes 5341184 | tf_op jit(solution)/shard_map/sd,cdn->csn/dot_general | solution.py:84
  251.9 0.2 fusion.66
  252.2 0.2 fusion.63
  252.4 0.2 fusion.64
  252.6 0.2 fusion.65
  252.9 3.0 convolution_convert_fusion
  255.9 0.7 copy-done.25
  256.7 1.8 fusion.31
  258.5 2.6 fusion.18
  261.3 1.7 collective-permute-start.5
  263.0 1.1 slice_bitcast_fusion.6
  264.2 1.0 collective-permute-start.6
  265.2 0.5 fusion.6
  265.8 1.2 add_convert_fusion.2
  266.9 3.4 %fusion.19 = f32[128,5120]{1,0:T(8,128)} fusion(bf16[2,128,5120]{2,1,0:T(8,128)(2,1)} %collective-permute-done, bf16[4,128,128]{1,2,0:T(8,128)(2,1)S(1)} %collective-permute-done.4), kind=kOutput, calls=%fused_computation.35 | convolution fusion | flops 167772160 | bytes 3964928 | tf_op jit(solution)/shard_map/sn,sd->nd/dot_general | solution.py:147
  270.3 2.5 fusion.21
  272.8 4.4 %fusion = bf16[1,1,3,5120,128]{3,4,2,1,0:T(8,128)(2,1)} fusion(f32[3,128,5120]{2,1,0:T(8,128)S(1)} %fusion.21, bf16[4,128,128]{1,2,0:T(8,128)(2,1)S(1)} %collective-permute-done.4, bf16[3,128,5120]{2,1,0:T(8,128)(2,1)S(1)} %add_convert_fusion.2, bf16[2,128,5120]{2,1,0:T(8,128)(2,1)} %collective-permute-done), kind=kOutput, calls=%fused_computation.6 | convolution fusion | flops 515112960 | bytes 17170432 | tf_op jit(solution)/shard_map/sd,csn->cdn/dot_general | solution.py:144
  277.3 6.3 %copy.18 = bf16[1,1,3,5120,128]{4,3,2,1,0:T(8,128)(2,1)} copy(bf16[1,1,3,5120,128]{3,4,2,1,0:T(8,128)(2,1)} %fusion) | data formatting | bytes 7864320
  283.5 11.9 %collective-permute-done.6 = bf16[128,5120]{1,0:T(8,128)(2,1)} collective-permute-done((bf16[128,5120]{1,0:T(8,128)(2,1)}, bf16[128,5120]{1,0:T(8,128)(2,1)}, u32[]{:S(2)}, u32[]{:S(2)}) %collective-permute-start.6) | collective-permute-done | bytes 1310752 | tf_op jit(solution)/shard_map/ppermute | solution.py:18
  295.4 3.8 %fusion.7 = bf16[1,1,128,5120]{3,2,1,0:T(8,128)(2,1)} fusion(f32[128,5120]{1,0:T(8,128)S(1)} %fusion.6, f32[128,5120]{1,0:T(8,128)} %fusion.19, bf16[128,5120]{1,0:T(8,128)(2,1)} %collective-permute-done.6, bf16[4,128,128]{1,2,0:T(8,128)(2,1)S(1)} %collective-permute-done.5), kind=kOutput, calls=%fused_computation.15 | convolution fusion | flops 171048960 | bytes 7897088 | tf_op jit(solution)/shard_map/sn,sd->nd/dot_general | solution.py:147
  299.2 7.9 %reduce-scatter.5.cloned.1.call-done = bf16[2,32,5120]{2,1,0:T(8,128)(2,1)} async-done(((bf16[2,128,5120]{2,1,0:T(8,128)(2,1)}), bf16[2,32,5120]{2,1,0:T(8,128)(2,1)}) %reduce-scatter.5.cloned.1.call-update) | async-done | bytes 655376 | tf_op jit(solution)/shard_map/reduce_scatter | solution.py:248
  307.1 1.2 fusion.88
  308.3 1.9 fusion.92
  310.2 0.9 maximum_bitcast_fusion.1
  311.1 0.9 maximum_bitcast_fusion
  (102 shorter events, 2.5 us)
Async XLA Ops:
  7.2 1.5 copy-start
  7.2 4.3 %copy-start.6 = (bf16[1,1,2,32,5120]{4,3,2,1,0:T(8,128)(2,1)S(1)}, bf16[1,1,2,32,5120]{4,3,2,1,0:T(8,128)(2,1)}, u32[]{:S(2)}) copy-start(bf16[1,1,2,32,5120]{4,3,2,1,0:T(8,128)(2,1)} %param.20) | copy-start | bytes 1966084
  7.2 4.3 %copy-start.21 = (f32[1,1,5120]{2,1,0:T(1,128)S(1)}, f32[1,1,5120]{2,1,0:T(1,128)}, u32[]{:S(2)}) copy-start(f32[1,1,5120]{2,1,0:T(1,128)} %param.15) | copy-start | bytes 61444
  7.2 5.4 %copy-start.17 = (bf16[1,1,32,5120]{3,2,1,0:T(8,128)(2,1)S(1)}, bf16[1,1,32,5120]{3,2,1,0:T(8,128)(2,1)}, u32[]{:S(2)}) copy-start(bf16[1,1,32,5120]{3,2,1,0:T(8,128)(2,1)} %param.19) | copy-start | bytes 983044
  7.2 5.4 %copy-start.12 = (bf16[1,2,32,5120]{3,2,1,0:T(8,128)(2,1)S(1)}, bf16[1,2,32,5120]{3,2,1,0:T(8,128)(2,1)}, u32[]{:S(2)}) copy-start(bf16[1,2,32,5120]{3,2,1,0:T(8,128)(2,1)} %param.21) | copy-start | bytes 1966084
  7.2 85.8 %all-gather.5.cloned.1.call-start = ((), (), s32[]{:S(2)}) async-start(), calls=%async_computation.2 | async-start | bytes 4915200 | tf_op jit(solution)/shard_map/all_gather | solution.py:52
  13.7 141.5 %reduce-scatter.3.cloned.1.call-start = ((), (), s32[]{:S(2)}) async-start(), calls=%async_computation.3 | async-start | bytes 3276800 | tf_op jit(solution)/shard_map/reduce_scatter | solution.py:248
  13.8 6.3 %copy-start.27 = (s32[1,2,5,128]{3,1,2,0:T(2,128)S(1)}, s32[1,2,5,128]{3,1,2,0:T(2,128)}, u32[]{:S(2)}) copy-start(s32[1,2,5,128]{3,1,2,0:T(2,128)} %param.13) | copy-start | bytes 15364
  93.0 4.8 %copy-start.13 = (bf16[1,1,128,5120]{3,2,1,0:T(8,128)(2,1)S(1)}, bf16[1,1,128,5120]{3,2,1,0:T(8,128)(2,1)}, u32[]{:S(2)}) copy-start(bf16[1,1,128,5120]{3,2,1,0:T(8,128)(2,1)} %param.17) | copy-start | bytes 3932164
  93.0 8.3 %copy-start.4 = (bf16[1,384,5120]{2,1,0:T(8,128)(2,1)S(1)}, bf16[1,384,5120]{2,1,0:T(8,128)(2,1)}, u32[]{:S(2)}) copy-start(bf16[1,384,5120]{2,1,0:T(8,128)(2,1)} %pad_bitcast_fusion) | copy-start | bytes 11796484
  97.6 3.6 %copy-start.26 = (bf16[2,3,128,128]{3,2,1,0:T(8,128)(2,1)}, bf16[2,3,128,128]{3,2,1,0:T(8,128)(2,1)S(1)}, u32[]{:S(2)}) copy-start(bf16[2,3,128,128]{3,2,1,0:T(8,128)(2,1)S(1)} %fusion.33) | copy-start | bytes 589828
  97.6 3.7 %copy-start.2 = (bf16[3,128,5120]{2,1,0:T(8,128)(2,1)S(1)}, bf16[3,128,5120]{2,1,0:T(8,128)(2,1)}, u32[]{:S(2)}) copy-start(bf16[3,128,5120]{2,1,0:T(8,128)(2,1)} %copy.15) | copy-start | bytes 11796484
  100.8 3.5 %copy-start.22 = (bf16[1,128,1,128]{1,3,2,0:T(8,128)(2,1)}, bf16[1,128,1,128]{1,3,2,0:T(8,128)(2,1)S(1)}, u32[]{:S(2)}) copy-start(bf16[1,128,1,128]{1,3,2,0:T(8,128)(2,1)S(1)} %fusion.61) | copy-start | bytes 98308
  104.3 85.2 %all-gather.9.cloned.1.call-start = ((), (), s32[]{:S(2)}) async-start(), calls=%async_computation.6 | async-start | bytes 1638400 | tf_op jit(solution)/shard_map/all_gather | solution.py:52
  109.1 60.3 %collective-permute-start = (bf16[2,128,5120]{2,1,0:T(8,128)(2,1)}, bf16[2,128,5120]{2,1,0:T(8,128)(2,1)}, u32[]{:S(2)}, u32[]{:S(2)}) collective-permute-start(bf16[2,128,5120]{2,1,0:T(8,128)(2,1)} %stack.115), channel_id=1, source_target_pairs={{0,25},{1,24},{8,17},{9,16},{16,9},{17,8},{24,1},{25,0},{2,27},{3,... | collective-permute-start | bytes 7864328 | tf_op jit(solution)/shard_map/ppermute | solution.py:18
  156.3 89.7 %all-gather.7.cloned.1.call-start = ((), (), s32[]{:S(2)}) async-start(), calls=%async_computation.4 | async-start | bytes 3276800 | tf_op jit(solution)/shard_map/all_gather | solution.py:52
  156.8 32.9 %copy-start.18 = (bf16[32,5120]{1,0:T(8,128)(2,1)}, bf16[32,5120]{1,0:T(8,128)(2,1)S(1)}, u32[]{:S(2)}) copy-start(bf16[32,5120]{1,0:T(8,128)(2,1)S(1)} %fusion.78) | copy-start | bytes 983044
  156.9 19.3 %collective-permute-start.1 = (bf16[32,5120]{1,0:T(8,128)(2,1)S(1)}, bf16[32,5120]{1,0:T(8,128)(2,1)S(1)}, u32[]{:S(2)}, u32[]{:S(2)}) collective-permute-start(bf16[32,5120]{1,0:T(8,128)(2,1)S(1)} %fusion.78), channel_id=1, source_target_pairs={{1,9},{8,0},{9,17},{16,8},{17,25},{24,16},{3,11},{10,2},{11,19},{1... | collective-permute-start | bytes 983048 | tf_op jit(solution)/shard_map/ppermute | solution.py:262
  159.2 30.3 %copy-start.15 = (bf16[32,5120]{1,0:T(8,128)(2,1)}, bf16[32,5120]{1,0:T(8,128)(2,1)S(1)}, u32[]{:S(2)}) copy-start(bf16[32,5120]{1,0:T(8,128)(2,1)S(1)} %fusion.90) | copy-start | bytes 983044
  159.2 16.9 %collective-permute-start.2 = (bf16[32,5120]{1,0:T(8,128)(2,1)S(1)}, bf16[32,5120]{1,0:T(8,128)(2,1)}, u32[]{:S(2)}, u32[]{:S(2)}) collective-permute-start(bf16[32,5120]{1,0:T(8,128)(2,1)S(1)} %fusion.90), channel_id=1, source_target_pairs={{0,8},{8,16},{9,1},{16,24},{17,9},{25,17},{2,10},{10,18},{11,3},{1... | collective-permute-start | bytes 983048 | tf_op jit(solution)/shard_map/ppermute | solution.py:263
  165.4 10.7 %copy-start.24 = (bf16[128,128]{1,0:T(8,128)(2,1)}, bf16[128,128]{1,0:T(8,128)(2,1)S(1)}, u32[]{:S(2)}) copy-start(bf16[128,128]{1,0:T(8,128)(2,1)S(1)} %convolution_convert_fusion.8) | copy-start | bytes 98308
  176.1 14.7 %copy-start.20 = (bf16[32,5120]{1,0:T(8,128)(2,1)}, bf16[32,5120]{1,0:T(8,128)(2,1)S(1)}, u32[]{:S(2)}) copy-start(bf16[32,5120]{1,0:T(8,128)(2,1)S(1)} %collective-permute-done.1) | copy-start | bytes 983044
  189.5 1.6 copy-start.8
  189.7 7.1 %copy-start.10 = (bf16[32,5120]{1,0:T(8,128)(2,1)}, bf16[32,5120]{1,0:T(8,128)(2,1)S(1)}, u32[]{:S(2)}) copy-start(bf16[32,5120]{1,0:T(8,128)(2,1)S(1)} %get-tuple-element.31) | copy-start | bytes 983044
  190.9 55.1 %copy-start.14 = (bf16[1,1,128,5120]{3,2,1,0:T(8,128)(2,1)S(1)}, bf16[1,1,128,5120]{3,2,1,0:T(8,128)(2,1)}, u32[]{:S(2)}) copy-start(bf16[1,1,128,5120]{3,2,1,0:T(8,128)(2,1)} %param.17) | copy-start | bytes 3932164
  190.9 116.2 %reduce-scatter.5.cloned.1.call-start = ((), (), s32[]{:S(2)}) async-start(), calls=%async_computation.5 | async-start | bytes 3276800 | tf_op jit(solution)/shard_map/reduce_scatter | solution.py:248
  191.1 64.8 %collective-permute-start.3 = (bf16[1,128,5120]{2,1,0:T(8,128)(2,1)S(1)}, bf16[1,128,5120]{2,1,0:T(8,128)(2,1)}, u32[]{:S(2)}, u32[]{:S(2)}) collective-permute-start(bf16[1,128,5120]{2,1,0:T(8,128)(2,1)S(1)} %bitcast.362), channel_id=1, source_target_pairs={{0,25},{1,24},{8,17},{9,16},{16,9},{17,8},{24,1},{25,0},{2,27},{3,... | collective-permute-start | bytes 3932168 | tf_op jit(solution)/shard_map/ppermute | solution.py:18
  192.3 63.6 %collective-permute-start.4 = (bf16[4,128,128]{1,2,0:T(8,128)(2,1)}, bf16[4,128,128]{1,2,0:T(8,128)(2,1)S(1)}, u32[]{:S(2)}, u32[]{:S(2)}) collective-permute-start(bf16[4,128,128]{1,2,0:T(8,128)(2,1)} %pad_maximum_fusion.5), channel_id=1, source_target_pairs={{0,25},{1,24},{8,17},{9,16},{16,9},{17,8},{24,1},{25,0},{2,27},{3,... | collective-permute-start | bytes 393224 | tf_op jit(solution)/shard_map/ppermute | solution.py:18
  246.0 6.9 %copy-start.5 = (bf16[1,384,5120]{2,1,0:T(8,128)(2,1)S(1)}, bf16[1,384,5120]{2,1,0:T(8,128)(2,1)}, u32[]{:S(2)}) copy-start(bf16[1,384,5120]{2,1,0:T(8,128)(2,1)} %pad_bitcast_fusion) | copy-start | bytes 11796484
  248.1 3.5 %copy-start.28 = (s32[128]{0:T(128)S(1)}, s32[128]{0:T(128)}, u32[]{:S(2)}) copy-start(s32[128]{0:T(128)} %get-tuple-element.65) | copy-start | bytes 1540
  248.1 4.7 %copy-start.3 = (bf16[3,128,5120]{2,1,0:T(8,128)(2,1)S(1)}, bf16[3,128,5120]{2,1,0:T(8,128)(2,1)}, u32[]{:S(2)}) copy-start(bf16[3,128,5120]{2,1,0:T(8,128)(2,1)} %copy.15) | copy-start | bytes 11796484
  255.9 0.8 copy-start.25
  256.6 1.8 copy-start.23
  258.5 4.6 %copy-start.11 = (bf16[2,128,5120]{2,1,0:T(8,128)(2,1)S(1)}, bf16[2,128,5120]{2,1,0:T(8,128)(2,1)}, u32[]{:S(2)}) copy-start(bf16[2,128,5120]{2,1,0:T(8,128)(2,1)} %all-gather.7.cloned.1.call-done) | copy-start | bytes 7864324
  261.3 9.0 %collective-permute-start.5 = (bf16[4,128,128]{1,2,0:T(8,128)(2,1)S(1)}, bf16[4,128,128]{1,2,0:T(8,128)(2,1)S(1)}, u32[]{:S(2)}, u32[]{:S(2)}) collective-permute-start(bf16[4,128,128]{1,2,0:T(8,128)(2,1)S(1)} %pad_maximum_fusion.6), channel_id=1, source_target_pairs={{0,25},{1,24},{8,17},{9,16},{16,9},{17,8},{24,1},{25,0},{2,27},{3,... | collective-permute-start | bytes 393224 | tf_op jit(solution)/shard_map/ppermute | solution.py:18
  264.2 1.6 copy-start.9
  264.2 31.3 %collective-permute-start.6 = (bf16[128,5120]{1,0:T(8,128)(2,1)}, bf16[128,5120]{1,0:T(8,128)(2,1)}, u32[]{:S(2)}, u32[]{:S(2)}) collective-permute-start(bf16[128,5120]{1,0:T(8,128)(2,1)} %slice_bitcast_fusion.6), channel_id=1, source_target_pairs={{0,25},{1,24},{8,17},{9,16},{16,9},{17,8},{24,1},{25,0},{2,27},{3,... | collective-permute-start | bytes 3932168 | tf_op jit(solution)/shard_map/ppermute | solution.py:18
  283.5 23.6 %copy-start.7 = (bf16[1,1,2,32,5120]{4,3,2,1,0:T(8,128)(2,1)S(1)}, bf16[1,1,2,32,5120]{4,3,2,1,0:T(8,128)(2,1)}, u32[]{:S(2)}) copy-start(bf16[1,1,2,32,5120]{4,3,2,1,0:T(8,128)(2,1)} %param.20) | copy-start | bytes 1966084
  299.2 11.0 %copy-start.19 = (bf16[32,5120]{1,0:T(8,128)(2,1)S(1)}, bf16[32,5120]{1,0:T(8,128)(2,1)}, u32[]{:S(2)}) copy-start(bf16[32,5120]{1,0:T(8,128)(2,1)} %copy-done.18) | copy-start | bytes 983044
  299.2 11.9 %copy-start.16 = (bf16[32,5120]{1,0:T(8,128)(2,1)S(1)}, bf16[32,5120]{1,0:T(8,128)(2,1)}, u32[]{:S(2)}) copy-start(bf16[32,5120]{1,0:T(8,128)(2,1)} %copy-done.15) | copy-start | bytes 983044
  308.3 3.7 %copy-start.1 = (bf16[64,5120]{1,0:T(8,128)(2,1)S(1)}, bf16[64,5120]{1,0:T(8,128)(2,1)}, u32[]{:S(2)}) copy-start(bf16[64,5120]{1,0:T(8,128)(2,1)} %param.14) | copy-start | bytes 1966084
Sparse Core Ops, SparseCore 0:
  13.8 79.1 all-gather.4
  104.4 50.7 reduce-scatter.2
  157.4 32.0 all-gather.8
  191.5 54.4 all-gather.6
  256.0 51.0 reduce-scatter.4
where the time goes:
time: 320 us; the launch traced here: 319 us
  waiting for transfers between devices  205 us (64%)
  matrix products  47.8 us (15%)
  local copies, waits for them, and re-layouts  24.6 us (8%)
  between operations  14.4 us (4%)
  starting transfers between devices  14.1 us (4%)
  other arithmetic  12.3 us (4%)
    all_gather x3, waiting for transfers between devices, gathered(): full = lax.all_gather(jnp.stack(blocks), 'tp', axis=1, tiled=True)  131 us
    reduce_scatter x2, waiting for transfers between devices, shards(): lax.psum_scatter(both_parts, 'tp', scatter_dimension=1, tiled=True)  52.4 us
    ppermute x5, waiting for transfers between devices, flipped(): lax.ppermute(value, axis, [(i, i ^ mask) for i in range(lax.axis_size(axi...  15.3 us
    dot_general x4, matrix products, weight_terms(): jnp.einsum('sd,csn->cdn', normed_full, d_projected, preferred_element_typ...  10.7 us
    dot_general x4, matrix products, weight_terms(): jnp.einsum('sn,sd->nd', mixed, upstream_full, preferred_element_type=jnp....  9.49 us
    unnamed x59, local copies, waits for them, and re-layouts  7.12 us
    ppermute x5, starting transfers between devices, flipped(): lax.ppermute(value, axis, [(i, i ^ mask) for i in range(lax.axis_size(axi...  7.08 us
    ppermute x1, waiting for transfers between devices, shards(): backward_in = lax.ppermute(backward_out, pair_axes, down_pairs)  6.69 us
  transfers between devices with their start and end apart: 12, of which 8 were waited for; matrix products, arithmetic and copies ran while one was open for 19% of the time, Pallas kernels for 0%

commit v1 on v0

--- a/solution.py
+++ b/solution.py
@@ -6,6 +6,18 @@
 from jax.sharding import PartitionSpec as P
 
 HD = 128
+
+
+def collect(x, axis, dim):
+    ways, here = (lax.axis_size(axis), lax.axis_index(axis))
+    grown, reach = (x, 1)
+    while reach < ways:
+        theirs = lax.ppermute(grown, axis, [(d, d ^ reach) for d in range(ways)])
+        mine_first = jnp.concatenate([grown, theirs], axis=dim)
+        theirs_first = jnp.concatenate([theirs, grown], axis=dim)
+        grown = jnp.where(here & reach == 0, mine_first, theirs_first)
+        reach = 2 * reach
+    return grown
 
 
 def passed_along(block, axis, distance):
@@ -49,7 +61,7 @@
 
 
 def gathered(blocks):
-    full = lax.all_gather(jnp.stack(blocks), "tp", axis=1, tiled=True)
+    full = collect(jnp.stack(blocks), "tp", 1)
     return [full[i] for i in range(len(blocks))]
 
 

time: 320 us -> 383 us (1.20)
  waiting for transfers between devices: 205 us -> 264 us
  matrix products: 47.8 us -> 38.2 us
  starting transfers between devices: 14.1 us -> 20.9 us
  other arithmetic: 12.3 us -> 17.5 us
    ppermute x0 -> x6, waiting for transfers between devices: none -> 200 us  [collect(): theirs = lax.ppermute(grown, axis, [(d, d ^ reach) for d in range(ways)])]
    all_gather x3 -> x0, waiting for transfers between devices: 131 us -> none  [gathered(): full = lax.all_gather(jnp.stack(blocks), 'tp', axis=1, tiled=True)]
    ppermute x0 -> x6, starting transfers between devices: none -> 9.72 us  [collect(): theirs = lax.ppermute(grown, axis, [(d, d ^ reach) for d in range(ways)])]
    select_n x0 -> x7, other arithmetic: none -> 7.67 us  [collect(): grown = jnp.where(here & reach == 0, mine_first, theirs_first)]
    ppermute x1, waiting for transfers between devices: 6.69 us -> 0.01 us  [shards(): backward_in = lax.ppermute(backward_out, pair_axes, down_pairs)]
    dot_general x2, matrix products: 6.45 us -> 1.73 us  [heads_of(): jnp.einsum('sd,cdn->csn', normed_full, qkv_weight, preferred_element_type...]
    ppermute x5, waiting for transfers between devices: 15.3 us -> 11 us  [flipped(): lax.ppermute(value, axis, [(i, i ^ mask) for i in range(lax.axis_size(axi...]
    unnamed x59 -> x95, local copies, waits for them, and re-layouts: 7.12 us -> 11.3 us
  transfers between devices with their start and end apart: 12 -> 15, of which waited for: 8 -> 9; matrix products, arithmetic and copies ran while one was open for 19% -> 14% of each run, Pallas kernels for 0% -> 0%
where the time goes in v1:
time: 383 us; the launch traced here: 382 us
  waiting for transfers between devices  264 us (69%)
  matrix products  38.2 us (10%)
  local copies, waits for them, and re-layouts  26.1 us (7%)
  starting transfers between devices  20.9 us (5%)
  other arithmetic  17.5 us (5%)
  between operations  14.9 us (4%)
    ppermute x6, waiting for transfers between devices, collect(): theirs = lax.ppermute(grown, axis, [(d, d ^ reach) for d in range(ways)])  200 us
    reduce_scatter x2, waiting for transfers between devices, shards(): lax.psum_scatter(both_parts, 'tp', scatter_dimension=1, tiled=True)  53.4 us
    unnamed x95, local copies, waits for them, and re-layouts  11.3 us
    ppermute x5, waiting for transfers between devices, flipped(): lax.ppermute(value, axis, [(i, i ^ mask) for i in range(lax.axis_size(axi...  11 us
    dot_general x4, matrix products, weight_terms(): jnp.einsum('sn,sd->nd', mixed, upstream_full, preferred_element_type=jnp....  10.8 us
    dot_general x4, matrix products, weight_terms(): jnp.einsum('sd,csn->cdn', normed_full, d_projected, preferred_element_typ...  10.8 us
    ppermute x6, starting transfers between devices, collect(): theirs = lax.ppermute(grown, axis, [(d, d ^ reach) for d in range(ways)])  9.72 us
    select_n x7, other arithmetic, collect(): grown = jnp.where(here & reach == 0, mine_first, theirs_first)  7.67 us
  transfers between devices with their start and end apart: 15, of which 9 were waited for; matrix products, arithmetic and copies ran while one was open for 14% of the time, Pallas kernels for 0%

profile of v1, /device:TPU:0, one launch (start us, length us, event | category | flops | bytes accessed | tf_op | source)
XLA Modules:
  0.0 381.8 jit_solution(5801120682936594483)
XLA Ops:
  7.3 0.8 slice_bitcast_fusion.59
  8.3 1.5 multiply_reduce_fusion
  9.8 1.5 fusion.69
  11.5 0.9 fusion.88
  12.5 0.8 copy-done.14
  13.4 3.1 collective-permute-start
  16.5 21.9 %collective-permute-done = bf16[3,32,5120]{2,1,0:T(8,128)(2,1)} collective-permute-done((bf16[3,32,5120]{2,1,0:T(8,128)(2,1)S(1)}, bf16[3,32,5120]{2,1,0:T(8,128)(2,1)}, u32[]{:S(2)}, u32[]{:S(2)}) %collective-permute-start) | collective-permute-done | bytes 983072 | tf_op jit(solution)/shard_map/ppermute | solution.py:15
  38.4 2.4 maximum_select_fusion.2
  40.8 2.8 collective-permute-start.1
  43.7 6.4 %copy.15 = bf16[3,128,5120]{2,1,0:T(8,128)(2,1)} copy(bf16[3,128,5120]{1,2,0:T(8,128)(2,1)} %bitcast.360) | data formatting | bytes 7864320 | tf_op jit(solution)/shard_map/transpose | solution.py:130
  50.1 1.7 pad_bitcast_fusion
  51.8 76.2 %collective-permute-done.1 = bf16[3,64,5120]{2,1,0:T(8,128)(2,1)} collective-permute-done((bf16[3,64,5120]{2,1,0:T(8,128)(2,1)S(1)}, bf16[3,64,5120]{2,1,0:T(8,128)(2,1)}, u32[]{:S(2)}, u32[]{:S(2)}) %collective-permute-start.1) | collective-permute-done | bytes 1966112 | tf_op jit(solution)/shard_map/ppermute | solution.py:15
  128.0 2.8 maximum_select_fusion
  130.9 1.6 fusion.32
  132.7 0.4 copy-done.23
  133.2 0.5 fusion.63
  135.3 3.0 convolution_convert_fusion.1
  138.4 1.0 copy-done.34
  139.4 0.3 fusion.9
  139.7 3.6 stack.115
  143.3 0.9 collective-permute-start.4
  144.3 0.9 convolution_convert_fusion.8
  145.2 0.7 pad_maximum_fusion.5
  145.9 45.9 %reduce-scatter.3.cloned.1.call-done = bf16[2,32,5120]{2,1,0:T(8,128)(2,1)} async-done(((bf16[2,128,5120]{2,1,0:T(8,128)(2,1)}), bf16[2,32,5120]{2,1,0:T(8,128)(2,1)}) %reduce-scatter.3.cloned.1.call-update) | async-done | bytes 655376 | tf_op jit(solution)/shard_map/reduce_scatter | solution.py:260
  191.8 1.1 slice_bitcast_fusion.24
  192.8 0.6 collective-permute-start.2
  194.0 1.3 collective-permute-start.5
  195.3 6.7 %collective-permute-done.2 = bf16[1,32,5120]{2,1,0:T(8,128)(2,1)S(1)} collective-permute-done((bf16[1,32,5120]{2,1,0:T(8,128)(2,1)S(1)}, bf16[1,32,5120]{2,1,0:T(8,128)(2,1)S(1)}, u32[]{:S(2)}, u32[]{:S(2)}) %collective-permute-start.2) | collective-permute-done | bytes 327712 | tf_op jit(solution)/shard_map/ppermute | solution.py:15
  202.1 2.4 collective-permute-start.3
  204.5 3.4 collective-permute-start.6
  208.1 24.4 %collective-permute-done.3 = bf16[1,64,5120]{2,1,0:T(8,128)(2,1)S(1)} collective-permute-done((bf16[1,64,5120]{2,1,0:T(8,128)(2,1)S(1)}, bf16[1,64,5120]{2,1,0:T(8,128)(2,1)S(1)}, u32[]{:S(2)}, u32[]{:S(2)}) %collective-permute-start.3) | collective-permute-done | bytes 655392 | tf_op jit(solution)/shard_map/ppermute | solution.py:15
  232.4 1.3 maximum_select_fusion.3
  234.1 0.4 copy-done.31
  235.1 16.6 %collective-permute-done.7 = bf16[2,32,5120]{2,1,0:T(8,128)(2,1)S(1)} collective-permute-done((bf16[2,32,5120]{2,1,0:T(8,128)(2,1)S(1)}, bf16[2,32,5120]{2,1,0:T(8,128)(2,1)S(1)}, u32[]{:S(2)}, u32[]{:S(2)}) %collective-permute-start.7) | collective-permute-done | bytes 655392 | tf_op jit(solution)/shard_map/ppermute | solution.py:15
  251.9 0.8 collective-permute-start.8
  252.7 0.6 collective-permute-start.9
  253.3 2.1 collective-permute-start.10
  255.4 0.8 fusion.41
  256.5 54.3 %collective-permute-done.8 = bf16[2,64,5120]{2,1,0:T(8,128)(2,1)S(1)} collective-permute-done((bf16[2,64,5120]{2,1,0:T(8,128)(2,1)S(1)}, bf16[2,64,5120]{2,1,0:T(8,128)(2,1)S(1)}, u32[]{:S(2)}, u32[]{:S(2)}) %collective-permute-start.8) | collective-permute-done | bytes 1310752 | tf_op jit(solution)/shard_map/ppermute | solution.py:15
  310.8 0.6 maximum_select_fusion.1
  311.5 0.5 fusion.62
  312.0 0.9 fusion.44
  314.7 0.4 copy-done.41
  315.0 0.7 copy-done.3
  315.7 3.0 convolution_convert_fusion
  318.8 1.8 fusion.30
  320.6 2.5 fusion.18
  323.1 1.0 convolution_convert_fusion.2
  324.1 1.9 collective-permute-start.11
  326.0 1.1 slice_bitcast_fusion.6
  327.2 0.9 collective-permute-start.12
  328.0 1.8 fusion.6
  329.9 1.3 add_convert_fusion.2
  331.2 3.4 fusion.20
  334.6 2.5 fusion.22
  337.1 4.5 %fusion = bf16[1,1,3,5120,128]{3,4,2,1,0:T(8,128)(2,1)} fusion(f32[3,128,5120]{2,1,0:T(8,128)S(1)} %fusion.22, bf16[4,128,128]{1,2,0:T(8,128)(2,1)} %collective-permute-done.10, bf16[3,128,5120]{2,1,0:T(8,128)(2,1)S(1)} %add_convert_fusion.2, bf16[2,128,5120]{2,1,0:T(8,128)(2,1)} %collective-permute-done.4), kind=kOutput, calls=%fused_computation.6 | convolution fusion | flops 515112960 | bytes 17170432 | tf_op jit(solution)/shard_map/sd,csn->cdn/dot_general | solution.py:156
  341.6 6.3 %copy.18 = bf16[1,1,3,5120,128]{4,3,2,1,0:T(8,128)(2,1)} copy(bf16[1,1,3,5120,128]{3,4,2,1,0:T(8,128)(2,1)} %fusion) | data formatting | bytes 7864320
  347.9 11.0 %collective-permute-done.12 = bf16[128,5120]{1,0:T(8,128)(2,1)} collective-permute-done((bf16[128,5120]{1,0:T(8,128)(2,1)}, bf16[128,5120]{1,0:T(8,128)(2,1)}, u32[]{:S(2)}, u32[]{:S(2)}) %collective-permute-start.12) | collective-permute-done | bytes 1310752 | tf_op jit(solution)/shard_map/ppermute | solution.py:30
  358.9 3.7 fusion.7
  362.6 7.5 %reduce-scatter.5.cloned.1.call-done = bf16[2,32,5120]{2,1,0:T(8,128)(2,1)} async-done(((bf16[2,128,5120]{2,1,0:T(8,128)(2,1)}), bf16[2,32,5120]{2,1,0:T(8,128)(2,1)}) %reduce-scatter.5.cloned.1.call-update) | async-done | bytes 655376 | tf_op jit(solution)/shard_map/reduce_scatter | solution.py:260
  370.1 1.2 fusion.85
  371.3 1.9 fusion.89
  373.2 0.9 maximum_bitcast_fusion.1
  374.1 0.9 maximum_bitcast_fusion
  (148 shorter events, 6.5 us)
Async XLA Ops:
  7.2 1.1 copy-start
  7.2 4.2 %copy-start.8 = (bf16[1,1,2,32,5120]{4,3,2,1,0:T(8,128)(2,1)S(1)}, bf16[1,1,2,32,5120]{4,3,2,1,0:T(8,128)(2,1)}, u32[]{:S(2)}) copy-start(bf16[1,1,2,32,5120]{4,3,2,1,0:T(8,128)(2,1)} %param.20) | copy-start | bytes 1966084
  7.2 4.2 %copy-start.32 = (f32[1,1,5120]{2,1,0:T(1,128)S(1)}, f32[1,1,5120]{2,1,0:T(1,128)}, u32[]{:S(2)}) copy-start(f32[1,1,5120]{2,1,0:T(1,128)} %param.15) | copy-start | bytes 61444
  7.2 5.2 %copy-start.27 = (bf16[1,1,32,5120]{3,2,1,0:T(8,128)(2,1)S(1)}, bf16[1,1,32,5120]{3,2,1,0:T(8,128)(2,1)}, u32[]{:S(2)}) copy-start(bf16[1,1,32,5120]{3,2,1,0:T(8,128)(2,1)} %param.19) | copy-start | bytes 983044
  7.2 5.2 %copy-start.21 = (bf16[1,2,32,5120]{3,2,1,0:T(8,128)(2,1)S(1)}, bf16[1,2,32,5120]{3,2,1,0:T(8,128)(2,1)}, u32[]{:S(2)}) copy-start(bf16[1,2,32,5120]{3,2,1,0:T(8,128)(2,1)} %param.21) | copy-start | bytes 1966084
  7.2 184.5 %reduce-scatter.3.cloned.1.call-start = ((), (), s32[]{:S(2)}) async-start(), calls=%async_computation.2 | async-start | bytes 3276800 | tf_op jit(solution)/shard_map/reduce_scatter | solution.py:260
  9.8 1.8 copy-start.10
  11.5 1.9 copy-start.15
  12.5 1.0 copy-start.16
  12.5 0.8 copy-start.14
  13.4 25.0 %collective-permute-start = (bf16[3,32,5120]{2,1,0:T(8,128)(2,1)S(1)}, bf16[3,32,5120]{2,1,0:T(8,128)(2,1)}, u32[]{:S(2)}, u32[]{:S(2)}) collective-permute-start(bf16[3,32,5120]{2,1,0:T(8,128)(2,1)S(1)} %pad_maximum_fusion.3), channel_id=1, source_target_pairs={{0,2},{2,0},{4,6},{6,4},{1,3},{3,1},{5,7},{7,5},{8,10},{10,8},{12,... | collective-permute-start | bytes 2949128 | tf_op jit(solution)/shard_map/ppermute | solution.py:15
  40.8 87.2 %collective-permute-start.1 = (bf16[3,64,5120]{2,1,0:T(8,128)(2,1)S(1)}, bf16[3,64,5120]{2,1,0:T(8,128)(2,1)}, u32[]{:S(2)}, u32[]{:S(2)}) collective-permute-start(bf16[3,64,5120]{2,1,0:T(8,128)(2,1)S(1)} %maximum_select_fusion.2), channel_id=1, source_target_pairs={{0,4},{2,6},{4,0},{6,2},{1,5},{3,7},{5,1},{7,3},{8,12},{10,14},{12... | collective-permute-start | bytes 5898248 | tf_op jit(solution)/shard_map/ppermute | solution.py:15
  43.7 6.4 %copy-start.46 = (s32[1,2,5,128]{3,1,2,0:T(2,128)S(1)}, s32[1,2,5,128]{3,1,2,0:T(2,128)}, u32[]{:S(2)}) copy-start(s32[1,2,5,128]{3,1,2,0:T(2,128)} %param.13) | copy-start | bytes 15364
  51.8 83.5 %copy-start.4 = (bf16[1,384,5120]{2,1,0:T(8,128)(2,1)}, bf16[1,384,5120]{2,1,0:T(8,128)(2,1)S(1)}, u32[]{:S(2)}) copy-start(bf16[1,384,5120]{2,1,0:T(8,128)(2,1)S(1)} %pad_bitcast_fusion) | copy-start | bytes 11796484
  51.8 79.0 %copy-start.12 = (bf16[1,1,3,5120,128]{4,3,2,1,0:T(8,128)(2,1)S(1)}, bf16[1,1,3,5120,128]{4,3,2,1,0:T(8,128)(2,1)}, u32[]{:S(2)}) copy-start(bf16[1,1,3,5120,128]{4,3,2,1,0:T(8,128)(2,1)} %param.16) | copy-start | bytes 11796484
  130.9 1.9 copy-start.6
  130.9 2.3 copy-start.23
  133.2 2.1 copy-start.45
  133.2 2.2 copy-start.2
  134.8 3.5 copy-start.39
  138.3 1.1 copy-start.34
  138.3 231.8 %reduce-scatter.5.cloned.1.call-start = ((), (), s32[]{:S(2)}) async-start(), calls=%async_computation.3 | async-start | bytes 3276800 | tf_op jit(solution)/shard_map/reduce_scatter | solution.py:260
  139.7 53.1 %copy-start.17 = (bf16[32,5120]{1,0:T(8,128)(2,1)S(1)}, bf16[32,5120]{1,0:T(8,128)(2,1)}, u32[]{:S(2)}) copy-start(bf16[32,5120]{1,0:T(8,128)(2,1)} %get-tuple-element.14) | copy-start | bytes 983044
  139.7 53.9 %copy-start.22 = (bf16[1,2,32,5120]{3,2,1,0:T(8,128)(2,1)S(1)}, bf16[1,2,32,5120]{3,2,1,0:T(8,128)(2,1)}, u32[]{:S(2)}) copy-start(bf16[1,2,32,5120]{3,2,1,0:T(8,128)(2,1)} %param.21) | copy-start | bytes 1966084
  139.7 53.9 %copy-start.28 = (bf16[1,1,32,5120]{3,2,1,0:T(8,128)(2,1)S(1)}, bf16[1,1,32,5120]{3,2,1,0:T(8,128)(2,1)}, u32[]{:S(2)}) copy-start(bf16[1,1,32,5120]{3,2,1,0:T(8,128)(2,1)} %param.19) | copy-start | bytes 983044
  143.3 61.1 %copy-start.11 = (f32[32,5120]{1,0:T(8,128)S(1)}, f32[32,5120]{1,0:T(8,128)}, u32[]{:S(2)}) copy-start(f32[32,5120]{1,0:T(8,128)} %copy-done.10) | copy-start | bytes 1966084
  143.3 90.4 %collective-permute-start.4 = (bf16[2,128,5120]{2,1,0:T(8,128)(2,1)}, bf16[2,128,5120]{2,1,0:T(8,128)(2,1)}, u32[]{:S(2)}, u32[]{:S(2)}) collective-permute-start(bf16[2,128,5120]{2,1,0:T(8,128)(2,1)} %stack.115), channel_id=1, source_target_pairs={{0,25},{1,24},{8,17},{9,16},{16,9},{17,8},{24,1},{25,0},{2,27},{3,... | collective-permute-start | bytes 7864328 | tf_op jit(solution)/shard_map/ppermute | solution.py:30
  145.2 59.3 %copy-start.43 = (bf16[128,128]{1,0:T(8,128)(2,1)}, bf16[128,128]{1,0:T(8,128)(2,1)S(1)}, u32[]{:S(2)}) copy-start(bf16[128,128]{1,0:T(8,128)(2,1)S(1)} %convolution_convert_fusion.8) | copy-start | bytes 98308
  191.8 12.7 %copy-start.33 = (bf16[2,32,5120]{2,1,0:T(8,128)(2,1)S(1)}, bf16[2,32,5120]{2,1,0:T(8,128)(2,1)}, u32[]{:S(2)}) copy-start(bf16[2,32,5120]{2,1,0:T(8,128)(2,1)} %reduce-scatter.3.cloned.1.call-done) | copy-start | bytes 1966084
  192.8 9.1 %collective-permute-start.2 = (bf16[1,32,5120]{2,1,0:T(8,128)(2,1)S(1)}, bf16[1,32,5120]{2,1,0:T(8,128)(2,1)S(1)}, u32[]{:S(2)}, u32[]{:S(2)}) collective-permute-start(bf16[1,32,5120]{2,1,0:T(8,128)(2,1)S(1)} %bitcast.361), channel_id=1, source_target_pairs={{0,2},{2,0},{4,6},{6,4},{1,3},{3,1},{5,7},{7,5},{8,10},{10,8},{12,... | collective-permute-start | bytes 983048 | tf_op jit(solution)/shard_map/ppermute | solution.py:15
  193.9 39.8 %copy-start.29 = (bf16[32,5120]{1,0:T(8,128)(2,1)}, bf16[32,5120]{1,0:T(8,128)(2,1)S(1)}, u32[]{:S(2)}) copy-start(bf16[32,5120]{1,0:T(8,128)(2,1)S(1)} %fusion.75) | copy-start | bytes 983044
  194.0 39.8 %collective-permute-start.5 = (bf16[32,5120]{1,0:T(8,128)(2,1)S(1)}, bf16[32,5120]{1,0:T(8,128)(2,1)S(1)}, u32[]{:S(2)}, u32[]{:S(2)}) collective-permute-start(bf16[32,5120]{1,0:T(8,128)(2,1)S(1)} %fusion.75), channel_id=1, source_target_pairs={{1,9},{8,0},{9,17},{16,8},{17,25},{24,16},{3,11},{10,2},{11,19},{1... | collective-permute-start | bytes 983048 | tf_op jit(solution)/shard_map/ppermute | solution.py:274
  202.1 30.4 %collective-permute-start.3 = (bf16[1,64,5120]{2,1,0:T(8,128)(2,1)S(1)}, bf16[1,64,5120]{2,1,0:T(8,128)(2,1)S(1)}, u32[]{:S(2)}, u32[]{:S(2)}) collective-permute-start(bf16[1,64,5120]{2,1,0:T(8,128)(2,1)S(1)} %maximum_select_fusion.7), channel_id=1, source_target_pairs={{0,4},{2,6},{4,0},{6,2},{1,5},{3,7},{5,1},{7,3},{8,12},{10,14},{12... | collective-permute-start | bytes 1966088 | tf_op jit(solution)/shard_map/ppermute | solution.py:15
  204.5 29.6 %copy-start.25 = (bf16[32,5120]{1,0:T(8,128)(2,1)}, bf16[32,5120]{1,0:T(8,128)(2,1)S(1)}, u32[]{:S(2)}) copy-start(bf16[32,5120]{1,0:T(8,128)(2,1)S(1)} %fusion.87) | copy-start | bytes 983044
  204.5 29.2 %collective-permute-start.6 = (bf16[32,5120]{1,0:T(8,128)(2,1)S(1)}, bf16[32,5120]{1,0:T(8,128)(2,1)S(1)}, u32[]{:S(2)}, u32[]{:S(2)}) collective-permute-start(bf16[32,5120]{1,0:T(8,128)(2,1)S(1)} %fusion.87), channel_id=1, source_target_pairs={{0,8},{8,16},{9,1},{16,24},{17,9},{25,17},{2,10},{10,18},{11,3},{1... | collective-permute-start | bytes 983048 | tf_op jit(solution)/shard_map/ppermute | solution.py:275
  232.4 22.9 %copy-start.19 = (bf16[1,64,5120]{2,1,0:T(8,128)(2,1)}, bf16[1,64,5120]{2,1,0:T(8,128)(2,1)S(1)}, u32[]{:S(2)}) copy-start(bf16[1,64,5120]{2,1,0:T(8,128)(2,1)S(1)} %collective-permute-done.3) | copy-start | bytes 1966084
  233.8 0.7 copy-start.31
  234.0 0.7 copy-start.18
  234.0 21.3 %copy-start.13 = (bf16[1,1,3,5120,128]{4,3,2,1,0:T(8,128)(2,1)S(1)}, bf16[1,1,3,5120,128]{4,3,2,1,0:T(8,128)(2,1)}, u32[]{:S(2)}) copy-start(bf16[1,1,3,5120,128]{4,3,2,1,0:T(8,128)(2,1)} %param.16) | copy-start | bytes 11796484
  235.0 16.7 %collective-permute-start.7 = (bf16[2,32,5120]{2,1,0:T(8,128)(2,1)S(1)}, bf16[2,32,5120]{2,1,0:T(8,128)(2,1)S(1)}, u32[]{:S(2)}, u32[]{:S(2)}) collective-permute-start(bf16[2,32,5120]{2,1,0:T(8,128)(2,1)S(1)} %pad_maximum_fusion.4), channel_id=1, source_target_pairs={{0,2},{2,0},{4,6},{6,4},{1,3},{3,1},{5,7},{7,5},{8,10},{10,8},{12,... | collective-permute-start | bytes 1966088 | tf_op jit(solution)/shard_map/ppermute | solution.py:15
  251.9 58.9 %collective-permute-start.8 = (bf16[2,64,5120]{2,1,0:T(8,128)(2,1)S(1)}, bf16[2,64,5120]{2,1,0:T(8,128)(2,1)S(1)}, u32[]{:S(2)}, u32[]{:S(2)}) collective-permute-start(bf16[2,64,5120]{2,1,0:T(8,128)(2,1)S(1)} %maximum_select_fusion.4), channel_id=1, source_target_pairs={{0,4},{2,6},{4,0},{6,2},{1,5},{3,7},{5,1},{7,3},{8,12},{10,14},{12... | collective-permute-start | bytes 3932168 | tf_op jit(solution)/shard_map/ppermute | solution.py:15
  252.7 66.0 %collective-permute-start.9 = (bf16[1,128,5120]{2,1,0:T(8,128)(2,1)}, bf16[1,128,5120]{2,1,0:T(8,128)(2,1)}, u32[]{:S(2)}, u32[]{:S(2)}) collective-permute-start(bf16[1,128,5120]{2,1,0:T(8,128)(2,1)} %maximum_select_fusion.3), channel_id=1, source_target_pairs={{0,25},{1,24},{8,17},{9,16},{16,9},{17,8},{24,1},{25,0},{2,27},{3,... | collective-permute-start | bytes 3932168 | tf_op jit(solution)/shard_map/ppermute | solution.py:30
  253.3 65.5 %collective-permute-start.10 = (bf16[4,128,128]{1,2,0:T(8,128)(2,1)}, bf16[4,128,128]{1,2,0:T(8,128)(2,1)}, u32[]{:S(2)}, u32[]{:S(2)}) collective-permute-start(bf16[4,128,128]{1,2,0:T(8,128)(2,1)} %pad_maximum_fusion.5), channel_id=1, source_target_pairs={{0,25},{1,24},{8,17},{9,16},{16,9},{17,8},{24,1},{25,0},{2,27},{3,... | collective-permute-start | bytes 393224 | tf_op jit(solution)/shard_map/ppermute | solution.py:30
  256.2 57.6 %copy-start.44 = (bf16[3,128,128]{2,1,0:T(8,128)(2,1)}, bf16[3,128,128]{2,1,0:T(8,128)(2,1)S(1)}, u32[]{:S(2)}) copy-start(bf16[3,128,128]{2,1,0:T(8,128)(2,1)S(1)} %fusion.41) | copy-start | bytes 294916
  256.5 55.0 %copy-start.24 = (bf16[1,1,128,5120]{3,2,1,0:T(8,128)(2,1)S(1)}, bf16[1,1,128,5120]{3,2,1,0:T(8,128)(2,1)}, u32[]{:S(2)}) copy-start(bf16[1,1,128,5120]{3,2,1,0:T(8,128)(2,1)} %param.17) | copy-start | bytes 3932164
  311.4 14.6 %copy-start.7 = (bf16[2,128,5120]{2,1,0:T(8,128)(2,1)}, bf16[2,128,5120]{2,1,0:T(8,128)(2,1)S(1)}, u32[]{:S(2)}) copy-start(bf16[2,128,5120]{2,1,0:T(8,128)(2,1)S(1)} %maximum_select_fusion.1) | copy-start | bytes 7864324
  311.5 3.6 copy-start.5
  312.0 3.7 copy-start.3
  313.8 0.6 copy-start.35
  314.1 0.6 copy-start.37
  314.4 0.6 copy-start.41
  318.8 1.8 copy-start.40
  324.1 10.5 %collective-permute-start.11 = (bf16[4,128,128]{1,2,0:T(8,128)(2,1)S(1)}, bf16[4,128,128]{1,2,0:T(8,128)(2,1)S(1)}, u32[]{:S(2)}, u32[]{:S(2)}) collective-permute-start(bf16[4,128,128]{1,2,0:T(8,128)(2,1)S(1)} %pad_maximum_fusion.6), channel_id=1, source_target_pairs={{0,25},{1,24},{8,17},{9,16},{16,9},{17,8},{24,1},{25,0},{2,27},{3,... | collective-permute-start | bytes 393224 | tf_op jit(solution)/shard_map/ppermute | solution.py:30
  327.2 2.7 copy-start.20
  327.2 2.7 copy-start.36
  327.2 2.7 copy-start.38
  327.2 2.7 copy-start.42
  327.2 31.7 %collective-permute-start.12 = (bf16[128,5120]{1,0:T(8,128)(2,1)}, bf16[128,5120]{1,0:T(8,128)(2,1)}, u32[]{:S(2)}, u32[]{:S(2)}) collective-permute-start(bf16[128,5120]{1,0:T(8,128)(2,1)} %slice_bitcast_fusion.6), channel_id=1, source_target_pairs={{0,25},{1,24},{8,17},{9,16},{16,9},{17,8},{24,1},{25,0},{2,27},{3,... | collective-permute-start | bytes 3932168 | tf_op jit(solution)/shard_map/ppermute | solution.py:30
  347.9 22.2 %copy-start.9 = (bf16[1,1,2,32,5120]{4,3,2,1,0:T(8,128)(2,1)S(1)}, bf16[1,1,2,32,5120]{4,3,2,1,0:T(8,128)(2,1)}, u32[]{:S(2)}) copy-start(bf16[1,1,2,32,5120]{4,3,2,1,0:T(8,128)(2,1)} %param.20) | copy-start | bytes 1966084
  362.6 10.6 %copy-start.30 = (bf16[32,5120]{1,0:T(8,128)(2,1)S(1)}, bf16[32,5120]{1,0:T(8,128)(2,1)}, u32[]{:S(2)}) copy-start(bf16[32,5120]{1,0:T(8,128)(2,1)} %copy-done.29) | copy-start | bytes 983044
  362.6 11.5 %copy-start.26 = (bf16[32,5120]{1,0:T(8,128)(2,1)S(1)}, bf16[32,5120]{1,0:T(8,128)(2,1)}, u32[]{:S(2)}) copy-start(bf16[32,5120]{1,0:T(8,128)(2,1)} %copy-done.25) | copy-start | bytes 983044
  371.3 3.7 copy-start.1
Sparse Core Ops, SparseCore 0:
  138.5 53.2 reduce-scatter.2
  318.9 51.1 reduce-scatter.4
